TPU v7x, 512 devices: a whole 4x4x16 slice. The times are simulated.
512 devices in a mesh: space: 64 (over z_lo, x, core), ky: 8 (over z_hi, y).
Axes of the slice: x: 4, y: 4, z: 16 (z_hi: 2, z_lo: 8; z = z_hi * 8 + z_lo), core: 2. Of those that a mesh axis runs over, the one named last changes fastest.
Arguments:
- distribution: float32 [64, 128, 256, 128], P('space', 'ky'), may hold values from 0 to 2
- region: int32 [64, 256], P('space'), may hold values from 0 to 5, as said below
- region_doping: float32 [6], replicated, may hold values from -1 to 2
- region_relax: float32 [6], replicated, may hold values from 0.2 to 1
- equilibrium: float32 [128, 128], P('ky'), may hold values from 0.3 to 3
- kx_speed: float32 [128], replicated, may hold values from 0.1 to 1
- upwind_sign: int32 [128], replicated, may hold values from -1 to 1, as said below
Outputs:
- advanced: float32 [64, 128, 256, 128], P('space', 'ky')
Inputs may be any that keep to these rules, and one draw needn't show every extreme that they name: region[x, y] = 2 band(y) + m[x, y], with m[x, y] 0 or 1 and band(y) = 0, 1, 2 on three runs of columns, each run at least 32 columns long. `upwind_sign`: exactly 64 entries are 1 and the others -1.
All inputs are finite; a program needn't handle non-finite values.
Results may differ from a plain program's by a relative error of at most 0.0003.
Values sent between devices are 32-bit elements; how exact they have to be, the bound alone decides.
No kernel may reach another device: no remote copies, remote signals or barrier semaphores. Data moves between devices by JAX's collectives and lax.ppermute only.
A program may use at most 64 MiB of HBM per device.

v0:
```python
import math
import jax
import jax.numpy as jnp
from jax import lax
from jax.sharding import PartitionSpec as P

COUPLING = 0.04
POISSON = 0.1
STEP = 0.4
DRIFT_Y = 0.8


def with_halo(block, sides, width):
    for axis, dim in sides:
        count = lax.axis_size(axis)
        forward = [(i, i + 1) for i in range(count - 1)]
        backward = [(target, source) for source, target in forward]
        low = lax.ppermute(
            lax.slice_in_dim(block, block.shape[dim] - width, None, axis=dim), axis, forward
        )
        high = lax.ppermute(lax.slice_in_dim(block, 0, width, axis=dim), axis, backward)
        block = jnp.concatenate([low, block, high], axis=dim)
    return block


def sine_table(length):
    positions = jnp.arange(1, length + 1, dtype=jnp.int32)
    phase_index = positions[:, None] * positions[None, :] % (2 * length + 2)
    return jnp.sqrt(2.0 / (length + 1.0)) * jnp.sin(
        math.pi * phase_index.astype(jnp.float32) / (length + 1.0)
    )


def eigen_values(length):
    positions = jnp.arange(1, length + 1, dtype=jnp.int32).astype(jnp.float32)
    return 4.0 * jnp.sin(0.5 * math.pi * positions / (length + 1.0)) ** 2


def wigner_tables(modes):
    half_count = modes // 2
    shifts = jnp.arange(1, half_count + 1, dtype=jnp.int32)
    wave_index = jnp.arange(modes, dtype=jnp.int32)
    phase_index = shifts[:, None] * wave_index[None, :] % modes
    angles = 2.0 * math.pi / modes * phase_index.astype(jnp.float32)
    forward = jnp.concatenate([jnp.cos(angles), jnp.sin(angles)], axis=0)
    backward = jnp.concatenate([jnp.sin(angles).T, -jnp.cos(angles).T], axis=1)
    return (forward, backward)


def own_differences(potential, modes, first_col, local_cols):
    half_count = modes // 2
    padded = jnp.pad(potential, ((0, 0), (half_count, half_count)))
    window = lax.dynamic_slice_in_dim(padded, first_col, local_cols + 2 * half_count, 1)
    pieces = []
    for offset in range(1, half_count + 1):
        ahead_vals = window[:, half_count + offset : half_count + offset + local_cols]
        behind = window[:, half_count - offset : half_count - offset + local_cols]
        pieces.append(ahead_vals - behind)
    return COUPLING * jnp.stack(pieces, axis=1)


def lookup(region, values_table):
    classes = jnp.arange(values_table.shape[0], dtype=jnp.int32)
    return jnp.sum(jnp.where(region[..., None] == classes, values_table, 0.0), axis=-1)


def shards(distribution, region, region_doping, region_relax, equilibrium, kx_speed, upwind_sign):
    precise = lax.Precision.HIGHEST
    triple = lax.Precision.HIGH
    row_count, ky_local, col_count, kx_count = distribution.shape
    ky_count = ky_local * lax.axis_size("ky")
    grid_rows = row_count * lax.axis_size("space")
    row_start = lax.axis_index("space") * row_count
    partial_value = jnp.sum(distribution, axis=(1, 3)) / (ky_count * kx_count)
    density = lax.psum(partial_value, "ky")
    doping = lookup(region, region_doping)
    relax_rate = lookup(region, region_relax)
    charge = density - doping
    sine_rows = sine_table(grid_rows)
    sine_cols = sine_table(col_count)
    eigen_cols = eigen_values(col_count)
    every_row = lax.all_gather(charge, "space", axis=0, tiled=True)
    along_x = jnp.dot(sine_rows, every_row, precision=precise)
    spectral = jnp.dot(along_x, sine_cols, precision=precise)
    spectral = spectral / (eigen_values(grid_rows)[:, None] + eigen_cols[None, :])
    back_cols = jnp.dot(spectral, sine_cols, precision=precise)
    own_rows = lax.dynamic_slice_in_dim(sine_rows, row_start, row_count, 0)
    potential = POISSON * jnp.dot(own_rows, back_cols, precision=precise)
    spread = lax.all_to_all(distribution, "ky", split_axis=2, concat_axis=1, tiled=True)
    local_cols = spread.shape[2]
    forward, backward = wigner_tables(ky_count)
    weights = own_differences(potential, ky_count, lax.axis_index("ky") * local_cols, local_cols)
    flattened = spread.reshape(row_count, ky_count, local_cols * kx_count)
    coeffs = jnp.einsum("ab,rbm->ram", forward, flattened, precision=triple)
    coeffs = coeffs.reshape(row_count, ky_count, local_cols, kx_count)
    scaled = coeffs * jnp.concatenate([weights, weights], axis=1)[..., None]
    mixed = jnp.einsum(
        "ab,rbm->ram",
        backward,
        scaled.reshape(row_count, ky_count, local_cols * kx_count),
        precision=triple,
    )
    mixed = mixed.reshape(row_count, ky_count, local_cols, kx_count)
    wigner = lax.all_to_all(mixed, "ky", split_axis=1, concat_axis=2, tiled=True)
    positive_kx = upwind_sign > 0
    padded = with_halo(distribution, (("space", 0),), 1)
    from_left = padded[:-2]
    from_right = padded[2:]
    upstream_x = jnp.where(positive_kx[None, None, None, :], from_left, from_right)
    drift_x = -kx_speed[None, None, None, :] * (distribution - upstream_x)
    ky_global = lax.axis_index("ky") * ky_local + jnp.arange(ky_local, dtype=jnp.int32)
    upward = ky_global >= ky_count // 2
    vertical = DRIFT_Y * (ky_global.astype(jnp.float32) + 0.5 - 0.5 * ky_count) / (0.5 * ky_count)
    zero_col = jnp.zeros_like(distribution[:, :, :1])
    from_low = jnp.concatenate([zero_col, distribution[:, :, :-1]], axis=2)
    from_high = jnp.concatenate([distribution[:, :, 1:], zero_col], axis=2)
    upstream_y = jnp.where(upward[None, :, None, None], from_low, from_high)
    drift_y = -jnp.abs(vertical)[None, :, None, None] * (distribution - upstream_y)
    relaxation = relax_rate[:, None, :, None] * (
        density[:, None, :, None] * equilibrium[None, :, None, :] - distribution
    )
    return distribution + STEP * (drift_x + drift_y + wigner + relaxation)


def solution(mesh):
    return jax.shard_map(
        shards,
        mesh=mesh,
        in_specs=(
            P("space", "ky", None, None),
            P("space", None),
            P(),
            P(),
            P("ky", None),
            P(),
            P(),
        ),
        out_specs=P("space", "ky", None, None),
        check_vma=False,
    )
```

profile of v0, /device:TPU:32, one launch (start us, length us, event | category | flops | bytes accessed | tf_op | source)
XLA Modules:
  0.0 378.6 jit_solution(6376607305004779924)
XLA Ops:
  0.0 4.1 %copy.28 = f32[1,16,256,128]{3,1,0,2:T(8,128)} copy(f32[1,16,256,128]{3,2,1,0:T(8,128)} %param.7) | data formatting | bytes 4194304 | tf_op args[0]
  4.1 17.0 %all-to-all-start = ((f32[1,16,256,128]{3,1,0,2:T(8,128)}), f32[1,16,256,128]{3,1,0,2:T(8,128)}, u32[]{:S(2)}, u32[]{:S(2)}) async-start(f32[1,16,256,128]{3,1,0,2:T(8,128)} %copy.28), calls=%async_computation | async-start | bytes 4194304 | tf_op jit(solution)/shard_map/all_to_all | solution.py:89
  21.1 0.2 reduce_sum.29
  21.3 117.8 %psum.7 = f32[1,256]{1,0:T(1,128)S(1)} all-reduce(f32[1,256]{1,0:T(1,128)S(1)} %bitcast.205), channel_id=1, replica_groups=mesh['space'=64,'ky'=8] {'ky'}, use_global_device_ids=true, to_apply=%region_1.0 | all-reduce | flops 256 | bytes 2048 | tf_op jit(solution)/shard_map/psum | solution.py:75
  139.2 0.1 fusion.65
  139.3 105.4 %all-gather = f32[64,1,256]{2,1,0:T(1,128)S(1)} all-gather(f32[1,1,256]{2,1,0:T(1,128)S(1)} %subtract_bitcast_fusion), channel_id=1, replica_groups=mesh['space'=64,'ky'=8] {'space'}, dimensions={0}, use_global_device_ids=true | all-gather | bytes 66560 | tf_op jit(solution)/shard_map/all_gather | solution.py:82
  244.7 0.2 fusion.53
  245.0 0.4 fusion.39
  245.3 1.3 convolution_divide_fusion
  246.7 1.3 fusion.14
  248.0 0.1 fusion.67
  248.2 0.1 fusion.180
  248.3 0.1 copy.84
  248.4 0.1 fusion.174
  248.5 0.1 copy.81
  248.6 0.1 fusion.184
  248.7 0.1 copy.86
  248.8 0.1 fusion.194
  248.9 0.1 copy.91
  249.0 0.1 fusion.196
  249.1 0.1 copy.92
  249.2 0.1 fusion.172
  249.4 0.1 copy.80
  249.4 0.1 fusion.178
  249.6 0.1 copy.83
  249.7 0.1 fusion.186
  249.8 0.1 copy.87
  249.9 0.1 fusion.182
  250.0 0.1 copy.85
  250.1 0.1 fusion.170
  250.2 0.1 copy.79
  250.3 0.1 fusion.192
  250.4 0.1 copy.90
  250.5 0.1 fusion.176
  250.6 0.1 copy.82
  250.7 0.1 fusion.188
  250.8 0.1 copy.88
  250.9 0.1 fusion.168
  251.0 0.1 copy.78
  251.1 0.1 fusion.190
  251.3 0.1 fusion.70
  252.4 0.1 copy.34
  253.0 0.1 copy.57
  254.1 0.1 copy.59
  254.7 0.1 copy.64
  255.7 0.3 stack.259
  256.2 0.1 copy.94
  256.3 1.9 mul.263
  258.2 2.7 mul.264
  260.9 0.2 fusion.62
  261.1 0.3 fusion.54
  261.5 2.4 copy.29
  263.8 2.2 fusion.1
  266.0 3.2 fusion.35
  269.2 3.1 copy.95
  272.3 7.1 %all-to-all-start.1 = ((f32[1,128,32,128]{3,2,0,1:T(8,128)}), f32[1,128,32,128]{3,2,0,1:T(8,128)}, u32[]{:S(2)}, u32[]{:S(2)}) async-start(f32[1,128,32,128]{3,2,0,1:T(8,128)} %copy.95), calls=%async_computation.1 | async-start | bytes 4194304 | tf_op jit(solution)/shard_map/all_to_all | solution.py:104
  279.4 2.4 collective-permute-start.1
  281.8 1.9 collective-permute-start
  283.9 2.5 fusion.209
  286.3 46.5 %all-to-all-done.1 = f32[1,128,32,128]{3,2,0,1:T(8,128)} async-done(((f32[1,128,32,128]{3,2,0,1:T(8,128)}), f32[1,128,32,128]{3,2,0,1:T(8,128)}, u32[]{:S(2)}, u32[]{:S(2)}) %all-to-all-start.1) | async-done | bytes 2097184 | tf_op jit(solution)/shard_map/all_to_all | solution.py:104
  332.9 2.0 copy.96
  334.8 29.5 %collective-permute-done.1 = f32[1,16,256,128]{3,2,1,0:T(8,128)} collective-permute-done((f32[1,16,256,128]{3,2,1,0:T(8,128)S(1)}, f32[1,16,256,128]{3,2,1,0:T(8,128)}, u32[]{:S(2)}, u32[]{:S(2)}) %collective-permute-start.1) | collective-permute-done | bytes 2097184 | tf_op jit(solution)/shard_map/ppermute | solution.py:21
  364.3 8.7 %collective-permute-done = f32[1,16,256,128]{3,2,1,0:T(8,128)} collective-permute-done((f32[1,16,256,128]{3,2,1,0:T(8,128)S(1)}, f32[1,16,256,128]{3,2,1,0:T(8,128)}, u32[]{:S(2)}, u32[]{:S(2)}) %collective-permute-start) | collective-permute-done | bytes 2097184 | tf_op jit(solution)/shard_map/ppermute | solution.py:18
  373.1 5.5 %fusion.6 = f32[1,16,256,128]{3,2,1,0:T(8,128)} fusion(f32[1,16,256,128]{3,2,1,0:T(8,128)S(1)} %copy-done, f32[1,16,8,32,128]{4,3,2,1,0:T(8,128)S(1)} %copy.96, f32[1,16,255,128]{3,2,1,0:T(8,128)S(1)} %copy-done.3, f32[1,16,255,128]{3,2,1,0:T(8,128)S(1)} %copy-done.2, f32[1,16,256,128]{3,2,1,0:T(8,128)} %collective-permute-done, ...), kind=kLoop, calls=%fused_computation.8 | loop fusion | flops 7340032 | bytes 14674640 | tf_op jit(solution)/shard_map/add | solution.py:122
  (80 shorter events, 4.3 us)
Async XLA Ops:
  4.1 17.0 %copy-start = (f32[1,16,256,128]{3,2,1,0:T(8,128)S(1)}, f32[1,16,256,128]{3,2,1,0:T(8,128)}, u32[]{:S(2)}) copy-start(f32[1,16,256,128]{3,2,1,0:T(8,128)} %param.7) | copy-start | bytes 6291460
  4.1 257.3 %all-to-all-start = ((f32[1,16,256,128]{3,1,0,2:T(8,128)}), f32[1,16,256,128]{3,1,0,2:T(8,128)}, u32[]{:S(2)}, u32[]{:S(2)}) async-start(f32[1,16,256,128]{3,1,0,2:T(8,128)} %copy.28), calls=%async_computation | async-start | bytes 4194304 | tf_op jit(solution)/shard_map/all_to_all | solution.py:89
  21.1 118.1 %copy-start.5 = (s32[1,256]{1,0:T(1,128)S(1)}, s32[1,256]{1,0:T(1,128)}, u32[]{:S(2)}) copy-start(s32[1,256]{1,0:T(1,128)} %param.8) | copy-start | bytes 3076
  21.1 118.1 %copy-start.6 = (f32[6]{0:T(128)S(1)}, f32[6]{0:T(128)}, u32[]{:S(2)}) copy-start(f32[6]{0:T(128)} %param.10) | copy-start | bytes 76
  21.1 118.0 %copy-start.7 = (f32[6]{0:T(128)S(1)}, f32[6]{0:T(128)}, u32[]{:S(2)}) copy-start(f32[6]{0:T(128)} %param.9) | copy-start | bytes 76
  261.4 2.4 copy-start.1
  272.3 11.4 %copy-start.8 = (f32[128]{0:T(128)S(1)}, f32[128]{0:T(128)}, u32[]{:S(2)}) copy-start(f32[128]{0:T(128)} %param.12) | copy-start | bytes 1540
  272.3 11.5 %copy-start.9 = (s32[128]{0:T(128)S(1)}, s32[128]{0:T(128)}, u32[]{:S(2)}) copy-start(s32[128]{0:T(128)} %param.13) | copy-start | bytes 1540
  272.3 60.5 %all-to-all-start.1 = ((f32[1,128,32,128]{3,2,0,1:T(8,128)}), f32[1,128,32,128]{3,2,0,1:T(8,128)}, u32[]{:S(2)}, u32[]{:S(2)}) async-start(f32[1,128,32,128]{3,2,0,1:T(8,128)} %copy.95), calls=%async_computation.1 | async-start | bytes 4194304 | tf_op jit(solution)/shard_map/all_to_all | solution.py:104
  279.4 84.9 %collective-permute-start.1 = (f32[1,16,256,128]{3,2,1,0:T(8,128)S(1)}, f32[1,16,256,128]{3,2,1,0:T(8,128)}, u32[]{:S(2)}, u32[]{:S(2)}) collective-permute-start(f32[1,16,256,128]{3,2,1,0:T(8,128)S(1)} %copy-done), channel_id=1, source_target_pairs={{8,0},{16,8},{24,16},{32,24},{40,32},{48,40},{56,48},{64,56},{72,6... | collective-permute-start | bytes 6291464 | tf_op jit(solution)/shard_map/ppermute | solution.py:21
  281.8 91.2 %collective-permute-start = (f32[1,16,256,128]{3,2,1,0:T(8,128)S(1)}, f32[1,16,256,128]{3,2,1,0:T(8,128)}, u32[]{:S(2)}, u32[]{:S(2)}) collective-permute-start(f32[1,16,256,128]{3,2,1,0:T(8,128)S(1)} %copy-done), channel_id=1, source_target_pairs={{0,8},{8,16},{16,24},{24,32},{32,40},{40,48},{48,56},{56,64},{64,7... | collective-permute-start | bytes 6291464 | tf_op jit(solution)/shard_map/ppermute | solution.py:18
  283.8 89.2 %copy-start.4 = (f32[16,128]{1,0:T(8,128)S(1)}, f32[16,128]{1,0:T(8,128)}, u32[]{:S(2)}) copy-start(f32[16,128]{1,0:T(8,128)} %param.11) | copy-start | bytes 24580
  332.9 40.2 %copy-start.2 = (f32[1,16,255,128]{3,2,1,0:T(8,128)S(1)}, f32[1,16,255,128]{3,2,1,0:T(8,128)}, u32[]{:S(2)}) copy-start(f32[1,16,255,128]{3,2,1,0:T(8,128)} %get-tuple-element.7) | copy-start | bytes 6266884
  332.9 40.2 %copy-start.3 = (f32[1,16,255,128]{3,2,1,0:T(8,128)S(1)}, f32[1,16,255,128]{3,2,1,0:T(8,128)}, u32[]{:S(2)}) copy-start(f32[1,16,255,128]{3,2,1,0:T(8,128)} %get-tuple-element.8) | copy-start | bytes 6266884
where the time goes:
time: 379 us
  blocking collectives  223 us (59%)
  waiting for transfers between devices  84.8 us (22%)
  starting transfers between devices  28.4 us (7%)
  local copies, waits for them, and re-layouts  24.8 us (7%)
  other arithmetic  8.64 us (2%)
  matrix products  8.58 us (2%)
    psum x1, blocking collectives, shards(): density = lax.psum(partial_value, 'ky')  118 us
    all_gather x1, blocking collectives, shards(): every_row = lax.all_gather(charge, 'space', axis=0, tiled=True)  105 us
    all_to_all x1, waiting for transfers between devices, shards(): lax.all_to_all(mixed, 'ky', split_axis=1, concat_axis=2, tiled=True)  46.5 us
    ppermute x1, waiting for transfers between devices, with_halo(): lax.ppermute(lax.slice_in_dim(block, 0, width, axis=dim), axis, backward)  29.5 us
    all_to_all x1, starting transfers between devices, shards(): lax.all_to_all(distribution, 'ky', split_axis=2, concat_axis=1, tiled=True)  17 us
    ppermute x1, waiting for transfers between devices, with_halo(): lax.ppermute(lax.slice_in_dim(block, block.shape[dim] - width, None, axis...  8.73 us
  transfers between devices with their start and end apart: 4, of which 3 were waited for; matrix products, arithmetic and copies ran while one was open for 6% of the time, Pallas kernels for 0%

commit v1 on v0

--- a/solution.py
+++ b/solution.py
@@ -101,7 +101,10 @@
         precision=triple,
     )
     mixed = mixed.reshape(row_count, ky_count, local_cols, kx_count)
-    wigner = lax.all_to_all(mixed, "ky", split_axis=1, concat_axis=2, tiled=True)
+    devices = lax.axis_size("ky")
+    blocks = jnp.stack(jnp.split(mixed, devices, axis=1), axis=0)
+    blocks = lax.all_to_all(blocks, "ky", split_axis=0, concat_axis=0)
+    wigner = jnp.concatenate(blocks, axis=2)
     positive_kx = upwind_sign > 0
     padded = with_halo(distribution, (("space", 0),), 1)
     from_left = padded[:-2]

time: 379 us -> 409 us (1.079)
  local copies, waits for them, and re-layouts: 24.8 us -> 56.2 us
    ppermute x1, waiting for transfers between devices: 8.73 us -> 39.6 us  [with_halo(): lax.ppermute(lax.slice_in_dim(block, block.shape[dim] - width, None, axis...]
    ppermute x1, waiting for transfers between devices: 29.5 us -> 0.01 us  [with_halo(): lax.ppermute(lax.slice_in_dim(block, 0, width, axis=dim), axis, backward)]
    unnamed x21 -> x36, local copies, waits for them, and re-layouts: 4.19 us -> 30.1 us
    split x0 -> x1, local copies, waits for them, and re-layouts: none -> 7.87 us  [shards(): blocks = jnp.stack(jnp.split(mixed, devices, axis=1), axis=0)]
    all_to_all x1, waiting for transfers between devices: 46.5 us -> 41.6 us  [shards(): blocks = lax.all_to_all(blocks, 'ky', split_axis=0, concat_axis=0)]
  transfers between devices with their start and end apart: 4 -> 4, of which waited for: 3 -> 2; matrix products, arithmetic and copies ran while one was open for 6% -> 5% of each run, Pallas kernels for 0% -> 0%
where the time goes in v1:
time: 409 us
  blocking collectives  223 us (55%)
  waiting for transfers between devices  81.2 us (20%)
  local copies, waits for them, and re-layouts  56.2 us (14%)
  starting transfers between devices  31.9 us (8%)
  other arithmetic  8.64 us (2%)
  matrix products  7.22 us (2%)
    psum x1, blocking collectives, shards(): density = lax.psum(partial_value, 'ky')  118 us
    all_gather x1, blocking collectives, shards(): every_row = lax.all_gather(charge, 'space', axis=0, tiled=True)  105 us
    all_to_all x1, waiting for transfers between devices, shards(): blocks = lax.all_to_all(blocks, 'ky', split_axis=0, concat_axis=0)  41.6 us
    ppermute x1, waiting for transfers between devices, with_halo(): lax.ppermute(lax.slice_in_dim(block, block.shape[dim] - width, None, axis...  39.6 us
    unnamed x36, local copies, waits for them, and re-layouts  30.1 us
    all_to_all x1, starting transfers between devices, shards(): lax.all_to_all(distribution, 'ky', split_axis=2, concat_axis=1, tiled=True)  17 us
  transfers between devices with their start and end apart: 4, of which 2 were waited for; matrix products, arithmetic and copies ran while one was open for 5% of the time, Pallas kernels for 0%

profile of v1, /device:TPU:32, one launch (start us, length us, event | category | flops | bytes accessed | tf_op | source)
XLA Modules:
  0.0 408.7 jit_solution(17277419159128647297)
XLA Ops:
  0.0 4.2 %copy.52 = f32[1,16,256,128]{3,1,0,2:T(8,128)} copy(f32[1,16,256,128]{3,2,1,0:T(8,128)} %param.7) | data formatting | bytes 4194304 | tf_op args[0]
  4.2 17.0 %all-to-all-start = ((f32[1,16,256,128]{3,1,0,2:T(8,128)}), f32[1,16,256,128]{3,1,0,2:T(8,128)}, u32[]{:S(2)}, u32[]{:S(2)}) async-start(f32[1,16,256,128]{3,1,0,2:T(8,128)} %copy.52), calls=%async_computation | async-start | bytes 4194304 | tf_op jit(solution)/shard_map/all_to_all | solution.py:89
  21.2 0.2 reduce_sum.29
  21.4 117.8 %psum.7 = f32[1,256]{1,0:T(1,128)S(1)} all-reduce(f32[1,256]{1,0:T(1,128)S(1)} %bitcast.220), channel_id=1, replica_groups=mesh['space'=64,'ky'=8] {'ky'}, use_global_device_ids=true, to_apply=%region_1.0 | all-reduce | flops 256 | bytes 2048 | tf_op jit(solution)/shard_map/psum | solution.py:75
  139.2 0.1 fusion.65
  139.3 105.4 %all-gather = f32[64,1,256]{2,1,0:T(1,128)S(1)} all-gather(f32[1,1,256]{2,1,0:T(1,128)S(1)} %subtract_bitcast_fusion), channel_id=1, replica_groups=mesh['space'=64,'ky'=8] {'space'}, dimensions={0}, use_global_device_ids=true | all-gather | bytes 66560 | tf_op jit(solution)/shard_map/all_gather | solution.py:82
  244.7 0.2 fusion.53
  245.0 0.4 fusion.39
  245.4 1.3 convolution_divide_fusion
  246.7 1.3 fusion.14
  248.1 0.1 fusion.67
  248.2 0.1 fusion.186
  248.4 0.1 fusion.194
  248.6 0.1 fusion.168
  248.7 0.1 copy.102
  248.8 0.1 fusion.170
  249.0 0.1 fusion.172
  249.2 0.1 fusion.174
  249.4 0.1 copy.105
  249.5 0.1 fusion.176
  249.7 0.1 fusion.178
  249.9 0.1 fusion.180
  250.1 0.1 fusion.182
  250.3 0.1 fusion.184
  250.6 0.1 fusion.188
  250.8 0.1 fusion.190
  251.0 0.1 fusion.192
  251.3 0.1 fusion.196
  251.4 0.1 copy.116
  255.3 0.1 fusion.70
  255.7 0.3 stack.286
  256.2 0.1 copy.118
  256.3 1.9 mul.263
  258.2 2.7 mul.264
  260.9 0.2 fusion.62
  261.2 0.3 fusion.54
  261.5 2.4 copy.53
  263.8 2.2 fusion.1
  266.0 1.8 fusion.35
  267.9 7.9 %fusion.210 = (f32[1,16,32,128]{1,3,2,0:T(8,128)}, f32[1,16,32,128]{1,3,2,0:T(8,128)}, f32[1,16,32,128]{1,3,2,0:T(8,128)}, f32[1,16,32,128]{1,3,2,0:T(8,128)}, f...) fusion(f32[1,128,32,128]{1,3,2,0:T(8,128)S(1)} %bitcast.199), kind=kLoop, calls=%fused_computation.371 | loop fusion | bytes 4194304 | tf_op jit(solution)/shard_map/split | solution.py:105
  275.7 2.2 copy.129
  277.9 0.7 bitcast_dynamic-update-slice_fusion.7
  278.7 2.9 copy.130
  281.6 2.9 copy.131
  284.5 2.2 copy.132
  286.7 2.2 copy.133
  288.9 2.2 copy.134
  291.1 2.2 copy.135
  293.3 2.2 copy.136
  295.5 1.7 bitcast_dynamic-update-slice_fusion.6
  297.2 1.7 bitcast_dynamic-update-slice_fusion.5
  298.9 0.7 bitcast_dynamic-update-slice_fusion.4
  299.6 0.7 bitcast_dynamic-update-slice_fusion.3
  300.3 0.7 bitcast_dynamic-update-slice_fusion.2
  301.0 0.7 bitcast_dynamic-update-slice_fusion.1
  301.7 0.7 bitcast_dynamic-update-slice_fusion
  302.4 7.1 %all-to-all-start.1 = ((f32[8,1,16,32,128]{4,3,2,1,0:T(8,128)}), f32[8,1,16,32,128]{4,3,2,1,0:T(8,128)}, u32[]{:S(2)}, u32[]{:S(2)}) async-start(f32[8,1,16,32,128]{4,3,2,1,0:T(8,128)} %bitcast_dynamic-update-slice_fusion), calls=%async_computation.1 | async-start | bytes 4194304 | tf_op jit(solution)/shard_map/all_to_all | solution.py:106
  309.5 1.9 collective-permute-start
  311.5 5.9 %collective-permute-start.1 = (f32[1,16,256,128]{3,2,1,0:T(8,128)S(1)}, f32[1,16,256,128]{3,2,1,0:T(8,128)}, u32[]{:S(2)}, u32[]{:S(2)}) collective-permute-start(f32[1,16,256,128]{3,2,1,0:T(8,128)S(1)} %copy-done), channel_id=1, source_target_pairs={{8,0},{16,8},{24,16},{32,24},{40,32},{48,40},{56,48},{64,56},{72,6... | collective-permute-start | bytes 6291464 | tf_op jit(solution)/shard_map/ppermute | solution.py:21
  317.5 2.5 fusion.209
  320.0 41.6 %all-to-all-done.1 = f32[8,1,16,32,128]{4,3,2,1,0:T(8,128)} async-done(((f32[8,1,16,32,128]{4,3,2,1,0:T(8,128)}), f32[8,1,16,32,128]{4,3,2,1,0:T(8,128)}, u32[]{:S(2)}, u32[]{:S(2)}) %all-to-all-start.1) | async-done | bytes 2097184 | tf_op jit(solution)/shard_map/all_to_all | solution.py:106
  361.6 2.0 copy.127
  363.6 39.6 %collective-permute-done = f32[1,16,256,128]{3,2,1,0:T(8,128)} collective-permute-done((f32[1,16,256,128]{3,2,1,0:T(8,128)S(1)}, f32[1,16,256,128]{3,2,1,0:T(8,128)}, u32[]{:S(2)}, u32[]{:S(2)}) %collective-permute-start) | collective-permute-done | bytes 2097184 | tf_op jit(solution)/shard_map/ppermute | solution.py:18
  403.2 5.5 %fusion.6 = f32[1,16,256,128]{3,2,1,0:T(8,128)} fusion(f32[1,16,256,128]{3,2,1,0:T(8,128)S(1)} %copy-done, f32[8,1,16,32,128]{4,3,0,2,1:T(8,128)S(1)} %copy.127, f32[1,16,255,128]{3,2,1,0:T(8,128)S(1)} %copy-done.3, f32[1,16,255,128]{3,2,1,0:T(8,128)S(1)} %copy-done.2, f32[1,16,256,128]{3,2,1,0:T(8,128)} %collective-permute-done, ...), kind=kLoop, calls=%fused_computation.8 | loop fusion | flops 7340032 | bytes 14674640 | tf_op jit(solution)/shard_map/add | solution.py:125
  (96 shorter events, 5.6 us)
Async XLA Ops:
  4.2 17.0 %copy-start = (f32[1,16,256,128]{3,2,1,0:T(8,128)S(1)}, f32[1,16,256,128]{3,2,1,0:T(8,128)}, u32[]{:S(2)}) copy-start(f32[1,16,256,128]{3,2,1,0:T(8,128)} %param.7) | copy-start | bytes 6291460
  4.2 257.3 %all-to-all-start = ((f32[1,16,256,128]{3,1,0,2:T(8,128)}), f32[1,16,256,128]{3,1,0,2:T(8,128)}, u32[]{:S(2)}, u32[]{:S(2)}) async-start(f32[1,16,256,128]{3,1,0,2:T(8,128)} %copy.52), calls=%async_computation | async-start | bytes 4194304 | tf_op jit(solution)/shard_map/all_to_all | solution.py:89
  21.1 118.1 %copy-start.5 = (s32[1,256]{1,0:T(1,128)S(1)}, s32[1,256]{1,0:T(1,128)}, u32[]{:S(2)}) copy-start(s32[1,256]{1,0:T(1,128)} %param.8) | copy-start | bytes 3076
  21.1 118.1 %copy-start.6 = (f32[6]{0:T(128)S(1)}, f32[6]{0:T(128)}, u32[]{:S(2)}) copy-start(f32[6]{0:T(128)} %param.10) | copy-start | bytes 76
  21.1 118.0 %copy-start.7 = (f32[6]{0:T(128)S(1)}, f32[6]{0:T(128)}, u32[]{:S(2)}) copy-start(f32[6]{0:T(128)} %param.9) | copy-start | bytes 76
  261.4 2.4 copy-start.1
  302.4 15.0 %copy-start.8 = (f32[128]{0:T(128)S(1)}, f32[128]{0:T(128)}, u32[]{:S(2)}) copy-start(f32[128]{0:T(128)} %param.12) | copy-start | bytes 1540
  302.4 15.0 %copy-start.9 = (s32[128]{0:T(128)S(1)}, s32[128]{0:T(128)}, u32[]{:S(2)}) copy-start(s32[128]{0:T(128)} %param.13) | copy-start | bytes 1540
  302.4 59.1 %all-to-all-start.1 = ((f32[8,1,16,32,128]{4,3,2,1,0:T(8,128)}), f32[8,1,16,32,128]{4,3,2,1,0:T(8,128)}, u32[]{:S(2)}, u32[]{:S(2)}) async-start(f32[8,1,16,32,128]{4,3,2,1,0:T(8,128)} %bitcast_dynamic-update-slice_fusion), calls=%async_computation.1 | async-start | bytes 4194304 | tf_op jit(solution)/shard_map/all_to_all | solution.py:106
  309.5 93.6 %collective-permute-start = (f32[1,16,256,128]{3,2,1,0:T(8,128)S(1)}, f32[1,16,256,128]{3,2,1,0:T(8,128)}, u32[]{:S(2)}, u32[]{:S(2)}) collective-permute-start(f32[1,16,256,128]{3,2,1,0:T(8,128)S(1)} %copy-done), channel_id=1, source_target_pairs={{0,8},{8,16},{16,24},{24,32},{32,40},{40,48},{48,56},{56,64},{64,7... | collective-permute-start | bytes 6291464 | tf_op jit(solution)/shard_map/ppermute | solution.py:18
  311.5 91.7 %collective-permute-start.1 = (f32[1,16,256,128]{3,2,1,0:T(8,128)S(1)}, f32[1,16,256,128]{3,2,1,0:T(8,128)}, u32[]{:S(2)}, u32[]{:S(2)}) collective-permute-start(f32[1,16,256,128]{3,2,1,0:T(8,128)S(1)} %copy-done), channel_id=1, source_target_pairs={{8,0},{16,8},{24,16},{32,24},{40,32},{48,40},{56,48},{64,56},{72,6... | collective-permute-start | bytes 6291464 | tf_op jit(solution)/shard_map/ppermute | solution.py:21
  317.5 85.7 %copy-start.4 = (f32[16,128]{1,0:T(8,128)S(1)}, f32[16,128]{1,0:T(8,128)}, u32[]{:S(2)}) copy-start(f32[16,128]{1,0:T(8,128)} %param.11) | copy-start | bytes 24580
  361.6 41.6 %copy-start.2 = (f32[1,16,255,128]{3,2,1,0:T(8,128)S(1)}, f32[1,16,255,128]{3,2,1,0:T(8,128)}, u32[]{:S(2)}) copy-start(f32[1,16,255,128]{3,2,1,0:T(8,128)} %get-tuple-element.7) | copy-start | bytes 6266884
  361.6 41.6 %copy-start.3 = (f32[1,16,255,128]{3,2,1,0:T(8,128)S(1)}, f32[1,16,255,128]{3,2,1,0:T(8,128)}, u32[]{:S(2)}) copy-start(f32[1,16,255,128]{3,2,1,0:T(8,128)} %get-tuple-element.8) | copy-start | bytes 6266884
